TPU v7x, 512 devices: a whole 4x8x8 slice. The times are simulated.
512 devices in a mesh: ep: 128 (over y, z, core), dp: 4 (over x).
Axes of the slice: x: 4, y: 8, z: 8, core: 2. Of those that a mesh axis runs over, the one named last changes fastest.
Arguments:
- tokens: bfloat16 [2, 2048, 3584], P(None, ('ep', 'dp')), may hold values from -6 to 6
- routing: int32 [2, 2048, 8], P(None, 'ep'), may hold values from 0 to 127, all different within a row; in each aligned block of 16 rows (0 to 15, 16 to 31, ..., all dimensions but the last counted through in order) at most 2 rows name the same one
- gate_values: float32 [2, 2048, 8], P(None, 'ep'), may hold values from 0.05 to 0.5
- held_weight: bfloat16 [128, 3584, 1024], P('ep', None, 'dp'), may hold values from -0.09375 to 0.09375
- scale_table: float32 [128, 28, 8], P(None, None, 'dp'), may hold values from 0.25 to 4
- old_expert: int32 [128], replicated, may hold values from 0 to 127, as said below
- new_expert: int32 [128], replicated, may hold values from 0 to 127, as said below
Outputs:
- combined: bfloat16 [2, 2048, 1024], P(None, 'ep', 'dp')
- moved_weight: bfloat16 [128, 3584, 1024], P('ep', None, 'dp')
Inputs may be any that keep to these rules, and one draw needn't show every extreme that they name: `routing`: each row names 8 different experts; in each aligned block of 16 token rows of a step no expert is named by more than 2 rows. `old_expert`: A permutation of the experts over the slots. `new_expert`: A permutation of the experts over the slots; it equals old_expert except at exactly 32 slots, whose experts are permuted among themselves so that each of them changes.
All inputs are finite; a program needn't handle non-finite values.
Results may differ from a plain program's by a relative error of at most 0.0039.
Values may be sent and summed in bfloat16 or wider, within the bound.
No kernel may reach another device: no remote copies, remote signals or barrier semaphores. Data moves between devices by JAX's collectives and lax.ppermute only.
A program may use at most 64 MiB of HBM per device.

v0:
```python
import jax
import jax.numpy as jnp
from jax import lax
from jax.sharding import PartitionSpec as P


def inverse_place(expert_at):
    count = expert_at.shape[0]
    labels = jnp.arange(count, dtype=jnp.int32)
    match = expert_at[None, :] == labels[:, None]
    return jnp.sum(jnp.where(match, labels[None, :], 0), axis=1)


def source_slots(old_expert, new_expert):
    labels = jnp.arange(old_expert.shape[0], dtype=jnp.int32)
    match = old_expert[None, :] == new_expert[:, None]
    return jnp.sum(jnp.where(match, labels[None, :], 0), axis=1)


def scaled_product(token_rows, weight_block, scales):
    row_blocks = scales.shape[0]
    block_rows = weight_block.shape[0] // row_blocks
    partial_value = jnp.einsum(
        "rbi,bif->rbf",
        token_rows.reshape(token_rows.shape[0], row_blocks, block_rows),
        weight_block.reshape(row_blocks, block_rows, weight_block.shape[1]),
        preferred_element_type=jnp.float32,
    )
    widened = jnp.repeat(scales, weight_block.shape[1] // scales.shape[1], axis=1)
    return jnp.sum(partial_value * widened[None, :, :], axis=1)


def expert_service(weight_block, scales):

    def serve_rows(arrived):

        def one_slot(slot_rows):
            return jax.nn.silu(scaled_product(slot_rows, weight_block, scales)).astype(jnp.bfloat16)

        activated = lax.map(one_slot, arrived)
        return lax.all_to_all(activated, "ep", split_axis=1, concat_axis=1, tiled=True)

    return serve_rows


def route_pairs(routing, expert_at, peers):
    pair_ids = routing.reshape(-1)
    labels = jnp.arange(peers, dtype=jnp.int32)
    onehot = (pair_ids[:, None] == labels[None, :]).astype(jnp.int32)
    before = jnp.cumsum(onehot, axis=0) - onehot
    slot_rank = jnp.sum(before * onehot, axis=1)
    owners = jnp.sum(onehot * inverse_place(expert_at)[None, :], axis=1)
    return slot_rank * peers + owners


def shards(tokens, routing, gate_values, held_weight, scale_table, old_expert, new_expert):
    peers = lax.axis_size("ep")
    my_slot = lax.axis_index("ep")
    group_size = routing.shape[1]
    top_count = routing.shape[2]
    capacity = min(group_size, max(2, 2 * group_size * top_count // peers))
    hidden_width = held_weight.shape[2]
    old_block = held_weight[0]
    sources = source_slots(old_expert, new_expert)
    pieces = old_block.reshape(peers, old_block.shape[0] // peers, hidden_width)
    new_block = lax.all_to_all(
        jnp.take(
            lax.all_to_all(pieces, "ep", split_axis=0, concat_axis=0, tiled=True), sources, axis=0
        ),
        "ep",
        split_axis=0,
        concat_axis=0,
        tiled=True,
    ).reshape(old_block.shape)
    first_serve = (new_block, new_expert)
    serve_plans = [first_serve] + [(new_block, new_expert)] * (tokens.shape[0] - 1)
    grouped = lax.all_gather(tokens, "dp", axis=1, tiled=True)
    columns = grouped.shape[2]
    combined_steps = []
    for decode_step in range(tokens.shape[0]):
        weight_block, expert_at = serve_plans[decode_step]
        scales = scale_table[expert_at[my_slot]]
        target = route_pairs(routing[decode_step], expert_at, peers)
        repeated = jnp.repeat(grouped[decode_step], top_count, axis=0)
        send_buffer = jnp.zeros((capacity * peers, columns), grouped.dtype).at[target].set(repeated)
        send_buffer = send_buffer.reshape(capacity, peers, columns)
        serve_rows = expert_service(weight_block, scales)
        returned = serve_rows(
            lax.all_to_all(send_buffer, "ep", split_axis=1, concat_axis=1, tiled=True)
        )
        activated = returned.reshape(capacity * peers, hidden_width)[target].astype(jnp.float32)
        activated = activated.reshape(group_size, top_count, hidden_width)
        weighted = jnp.sum(gate_values[decode_step][:, :, None] * activated, axis=1)
        combined_steps.append(weighted.astype(jnp.bfloat16))
    return (jnp.stack(combined_steps), new_block[None])


def solution(mesh):
    placed = (
        P(None, ("ep", "dp"), None),
        P(None, "ep", None),
        P(None, "ep", None),
        P("ep", None, "dp"),
        P(None, None, "dp"),
        P(),
        P(),
    )
    return jax.shard_map(
        shards,
        mesh=mesh,
        in_specs=placed,
        out_specs=(P(None, "ep", "dp"), P("ep", None, "dp")),
        check_vma=False,
    )
```

profile of v0, /device:TPU:1, one launch (start us, length us, event | category | flops | bytes accessed | tf_op | source)
XLA Modules:
  0.0 315.5 jit_solution(4355905081281846887)
XLA Ops:
  0.6 0.7 fusion.26
  1.4 0.1 eq.32
  1.5 0.1 fusion.21
  1.7 0.1 eq.79
  1.8 0.1 fusion.20
  1.9 0.2 reduce_window_sum.17
  2.0 0.2 reduce_window_sum.18
  2.2 0.9 copy.58
  3.1 10.5 %all_gather.3 = bf16[2,16,3584]{2,0,1:T(2,128)(2,1)S(1)} all-gather(bf16[2,4,3584]{2,0,1:T(2,128)(2,1)S(1)} %copy.58), channel_id=1, replica_groups=mesh['ep'=128,'dp'=4] {'dp'}, dimensions={1}, use_global_device_ids=true | all-gather | bytes 286720 | tf_op jit(solution)/shard_map/all_gather | solution.py:77
  13.6 0.3 fusion.25
  13.9 0.9 select_reduce_fusion.2
  14.8 0.2 select_reduce_fusion.5
  15.1 2.5 scatter_custom_fusion
  17.5 3.1 copy.60
  20.7 20.5 %all-to-all-start = ((bf16[2,128,3584]{2,0,1:T(2,128)(2,1)}), bf16[2,128,3584]{2,0,1:T(2,128)(2,1)S(1)}, u32[]{:S(2)}, u32[]{:S(2)}) async-start(bf16[2,128,3584]{2,0,1:T(2,128)(2,1)} %copy.60), calls=%async_computation | async-start | bytes 3670016 | tf_op jit(solution)/shard_map/all_to_all | solution.py:89
  41.1 3.7 %reshape_squeeze.3 = bf16[128,28,256]{2,1,0:T(8,128)(2,1)} reshape(bf16[1,3584,256]{2,1,0:T(8,128)(2,1)} %param.14) | data formatting | bytes 3670016 | tf_op jit(solution)/shard_map/reshape;squeeze | solution.py:65
  44.9 42.7 %all-to-all-done = bf16[2,128,3584]{2,0,1:T(2,128)(2,1)S(1)} async-done(((bf16[2,128,3584]{2,0,1:T(2,128)(2,1)}), bf16[2,128,3584]{2,0,1:T(2,128)(2,1)S(1)}, u32[]{:S(2)}, u32[]{:S(2)}) %all-to-all-start) | async-done | bytes 1835040 | tf_op jit(solution)/shard_map/all_to_all | solution.py:89
  87.6 1.3 copy-done.3
  88.9 7.8 %all-to-all-start.1 = ((bf16[128,28,256]{2,1,0:T(8,128)(2,1)}), bf16[128,28,256]{2,1,0:T(8,128)(2,1)S(1)}, u32[]{:S(2)}, u32[]{:S(2)}) async-start(bf16[128,28,256]{2,1,0:T(8,128)(2,1)} %reshape_squeeze.3), calls=%async_computation.1 | async-start | bytes 4194304 | tf_op jit(solution)/shard_map/all_to_all | solution.py:68
  96.7 3.3 %scatter_custom_fusion.1 = bf16[256,3584]{1,0:T(8,128)(2,1)} fusion(s32[128]{0:T(128)S(1)} %get-tuple-element.141, bf16[]{:T(256)} %constant.58.clone.1, bf16[16,3584]{1,0:T(8,128)(2,1)S(1)} %get-tuple-element.142), kind=kCustom, calls=%fused_computation.24 | custom fusion | bytes 1949698 | tf_op jit(solution)/shard_map/scatter | solution.py:85
  100.0 4.6 %copy.69 = bf16[2,128,3584]{2,0,1:T(2,128)(2,1)} copy(bf16[2,128,3584]{2,1,0:T(8,128)(2,1)} %bitcast.125) | data formatting | bytes 3670016 | tf_op jit(solution)/shard_map/reshape | solution.py:86
  104.6 44.2 %all-to-all-done.1 = bf16[128,28,256]{2,1,0:T(8,128)(2,1)S(1)} async-done(((bf16[128,28,256]{2,1,0:T(8,128)(2,1)}), bf16[128,28,256]{2,1,0:T(8,128)(2,1)S(1)}, u32[]{:S(2)}, u32[]{:S(2)}) %all-to-all-start.1) | async-done | bytes 1835040 | tf_op jit(solution)/shard_map/all_to_all | solution.py:68
  148.8 8.1 %all-to-all-start.4 = ((bf16[2,128,3584]{2,0,1:T(2,128)(2,1)}), bf16[2,128,3584]{2,0,1:T(2,128)(2,1)}, u32[]{:S(2)}, u32[]{:S(2)}) async-start(bf16[2,128,3584]{2,0,1:T(2,128)(2,1)} %copy.69), calls=%async_computation.4 | async-start | bytes 3670016 | tf_op jit(solution)/shard_map/all_to_all | solution.py:89
  157.0 2.0 gather_fusion
  159.0 3.2 %broadcast_select_fusion = bf16[128,28,256]{2,1,0:T(8,128)(2,1)} fusion(bf16[128,28,256]{2,1,0:T(8,128)(2,1)} %gather_fusion, pred[128]{0:T(512)(128)(4,1)S(1)} %compare_and_fusion), kind=kLoop, calls=%fused_computation.23 | loop fusion | flops 917504 | bytes 3670144 | tf_op jit(solution)/shard_map/jit(_take)/select_n | solution.py:67
  162.2 40.9 %all-to-all-done.4 = bf16[2,128,3584]{2,0,1:T(2,128)(2,1)} async-done(((bf16[2,128,3584]{2,0,1:T(2,128)(2,1)}), bf16[2,128,3584]{2,0,1:T(2,128)(2,1)}, u32[]{:S(2)}, u32[]{:S(2)}) %all-to-all-start.4) | async-done | bytes 1835040 | tf_op jit(solution)/shard_map/all_to_all | solution.py:89
  203.1 7.8 %all-to-all-start.2 = ((bf16[128,28,256]{2,1,0:T(8,128)(2,1)}), bf16[128,28,256]{2,1,0:T(8,128)(2,1)S(1)}, u32[]{:S(2)}, u32[]{:S(2)}) async-start(bf16[128,28,256]{2,1,0:T(8,128)(2,1)} %broadcast_select_fusion), calls=%async_computation.2 | async-start | bytes 4194304 | tf_op jit(solution)/shard_map/all_to_all | solution.py:66
  210.9 0.6 dynamic_slice.15
  213.5 0.1 constant_dynamic-slice_fusion.2
  213.6 0.1 copy.61
  213.7 0.1 copy.63
  213.8 5.6 %copy.62 = bf16[2,128,3584]{1,2,0:T(8,128)(2,1)} copy(bf16[2,128,3584]{2,0,1:T(2,128)(2,1)} %copy-done.3) | data formatting | bytes 3670016 | tf_op jit(solution)/shard_map/while | solution.py:40
  219.3 5.5 %copy.70 = bf16[2,128,3584]{1,2,0:T(8,128)(2,1)} copy(bf16[2,128,3584]{2,0,1:T(2,128)(2,1)} %all-to-all-done.4) | data formatting | bytes 3670016 | tf_op jit(solution)/shard_map/while | solution.py:40
  224.9 38.2 %all-to-all-done.2 = bf16[128,28,256]{2,1,0:T(8,128)(2,1)S(1)} async-done(((bf16[128,28,256]{2,1,0:T(8,128)(2,1)}), bf16[128,28,256]{2,1,0:T(8,128)(2,1)S(1)}, u32[]{:S(2)}, u32[]{:S(2)}) %all-to-all-start.2) | async-done | bytes 1835040 | tf_op jit(solution)/shard_map/all_to_all | solution.py:66
  263.1 1.5 reshape_reshape.6
  264.6 0.4 copy-done.1
  265.0 5.2 %while.22 = (s32[]{:T(128)}, bf16[2,128,256]{2,1,0:T(8,128)(2,1)S(1)}, bf16[2,128,3584]{1,2,0:T(8,128)(2,1)}, bf16[128,28,256]{2,1,0:T(8,128)(2,1)}, f32[28,2]{1...) while((s32[]{:T(128)}, bf16[2,128,256]{2,1,0:T(8,128)(2,1)S(1)}, ...), condition=%wide.wide.region_8.9_spmd, body=%wide.wide.region_6.8_spmd.sunk | while | flops 236847104 | bytes 12439901 | solution.py:40
  265.0 1.4 constant_dynamic-slice_fusion.7
  266.4 0.1 broadcast_in_dim.76
  266.5 0.3 copy-done.5
  266.8 0.7 multiply_reduce_fusion.6
  267.6 1.4 constant_dynamic-slice_fusion.7
  269.0 0.1 broadcast_in_dim.76
  269.1 0.3 copy-done.5
  269.4 0.7 multiply_reduce_fusion.6
  270.2 0.8 copy.64
  270.9 7.7 %all-to-all-start.3 = ((bf16[2,128,256]{2,0,1:T(2,128)(2,1)}), bf16[2,128,256]{2,0,1:T(2,128)(2,1)S(1)}, u32[]{:S(2)}, u32[]{:S(2)}) async-start(bf16[2,128,256]{2,0,1:T(2,128)(2,1)} %copy.64), calls=%async_computation.3 | async-start | bytes 262144 | tf_op jit(solution)/shard_map/all_to_all | solution.py:41
  278.7 3.9 %reshape_reshape.8 = bf16[28,128,256]{2,1,0:T(8,128)(2,1)} reshape(bf16[128,28,256]{2,1,0:T(8,128)(2,1)} %get-tuple-element.307) | data formatting | bytes 3670016 | tf_op jit(solution)/shard_map/while/body/eval_jaxpr/reshape;reshape | solution.py:26
  282.6 4.6 %while.23 = (s32[]{:T(128)}, bf16[2,128,256]{2,1,0:T(8,128)(2,1)S(1)}, bf16[2,128,3584]{1,2,0:T(8,128)(2,1)S(1)}, bf16[128,28,256]{2,1,0:T(8,128)(2,1)}, f32[28,...) while((s32[]{:T(128)}, bf16[2,128,256]{2,1,0:T(8,128)(2,1)S(1)}, ...), condition=%wide.wide.region_16.17_spmd, body=%wide.wide.region_14.16_spmd.sunk | while | flops 236847104 | bytes 12439901 | solution.py:40
  282.7 0.1 broadcast_in_dim.77
  282.8 1.3 copy-done.4
  284.1 0.7 multiply_reduce_fusion.7
  285.1 1.3 copy-done.4
  286.4 0.7 multiply_reduce_fusion.7
  287.2 0.8 copy.72
  288.0 3.0 all-to-all-done.3
  290.9 10.8 %all-to-all-start.5 = ((bf16[2,128,256]{2,0,1:T(2,128)(2,1)}), bf16[2,128,256]{2,0,1:T(2,128)(2,1)S(1)}, u32[]{:S(2)}, u32[]{:S(2)}) async-start(bf16[2,128,256]{2,0,1:T(2,128)(2,1)} %copy.72), calls=%async_computation.5 | async-start | bytes 262144 | tf_op jit(solution)/shard_map/all_to_all | solution.py:41
  301.9 3.7 %broadcast_in_dim_reshape.3 = bf16[1,3584,256]{2,1,0:T(8,128)(2,1)} reshape(bf16[128,28,256]{2,1,0:T(8,128)(2,1)} %get-tuple-element.308) | data formatting | bytes 3670016 | tf_op jit(solution)/shard_map/broadcast_in_dim;reshape | solution.py:95
  305.6 0.8 gather_fusion.1
  306.5 0.1 fusion.19
  306.6 7.3 %all-to-all-done.5 = bf16[2,128,256]{2,0,1:T(2,128)(2,1)S(1)} async-done(((bf16[2,128,256]{2,0,1:T(2,128)(2,1)}), bf16[2,128,256]{2,0,1:T(2,128)(2,1)S(1)}, u32[]{:S(2)}, u32[]{:S(2)}) %all-to-all-start.5) | async-done | bytes 131104 | tf_op jit(solution)/shard_map/all_to_all | solution.py:41
  313.9 0.8 gather_fusion.2
  314.7 0.1 fusion.18
  314.9 0.6 pad_maximum_fusion
  (45 shorter events, 0.9 us)
Async XLA Ops:
  0.6 212.8 %copy-start = (f32[128,28,2]{0,2,1:T(2,128)S(1)}, f32[128,28,2]{0,2,1:T(2,128)}, u32[]{:S(2)}) copy-start(f32[128,28,2]{0,2,1:T(2,128)} %param.15) | copy-start | bytes 86020
  20.7 67.0 %all-to-all-start = ((bf16[2,128,3584]{2,0,1:T(2,128)(2,1)}), bf16[2,128,3584]{2,0,1:T(2,128)(2,1)S(1)}, u32[]{:S(2)}, u32[]{:S(2)}) async-start(bf16[2,128,3584]{2,0,1:T(2,128)(2,1)} %copy.60), calls=%async_computation | async-start | bytes 3670016 | tf_op jit(solution)/shard_map/all_to_all | solution.py:89
  87.6 1.3 copy-start.3
  88.9 59.9 %all-to-all-start.1 = ((bf16[128,28,256]{2,1,0:T(8,128)(2,1)}), bf16[128,28,256]{2,1,0:T(8,128)(2,1)S(1)}, u32[]{:S(2)}, u32[]{:S(2)}) async-start(bf16[128,28,256]{2,1,0:T(8,128)(2,1)} %reshape_squeeze.3), calls=%async_computation.1 | async-start | bytes 4194304 | tf_op jit(solution)/shard_map/all_to_all | solution.py:68
  148.8 54.3 %all-to-all-start.4 = ((bf16[2,128,3584]{2,0,1:T(2,128)(2,1)}), bf16[2,128,3584]{2,0,1:T(2,128)(2,1)}, u32[]{:S(2)}, u32[]{:S(2)}) async-start(bf16[2,128,3584]{2,0,1:T(2,128)(2,1)} %copy.69), calls=%async_computation.4 | async-start | bytes 3670016 | tf_op jit(solution)/shard_map/all_to_all | solution.py:89
  162.2 48.7 %copy-start.7 = (s32[128]{0:T(128)S(1)}, s32[128]{0:T(128)}, u32[]{:S(2)}) copy-start(s32[128]{0:T(128)} %param.17) | copy-start | bytes 1540
  162.2 51.5 %copy-start.6 = (f32[2,16,8]{1,2,0:T(8,128)S(1)}, f32[2,16,8]{1,2,0:T(8,128)}, u32[]{:S(2)}) copy-start(f32[2,16,8]{1,2,0:T(8,128)} %param.13) | copy-start | bytes 3076
  203.1 59.9 %all-to-all-start.2 = ((bf16[128,28,256]{2,1,0:T(8,128)(2,1)}), bf16[128,28,256]{2,1,0:T(8,128)(2,1)S(1)}, u32[]{:S(2)}, u32[]{:S(2)}) async-start(bf16[128,28,256]{2,1,0:T(8,128)(2,1)} %broadcast_select_fusion), calls=%async_computation.2 | async-start | bytes 4194304 | tf_op jit(solution)/shard_map/all_to_all | solution.py:66
  263.1 1.9 copy-start.1
  265.0 1.8 copy-start.5
  267.6 1.8 copy-start.5
  270.9 20.0 %all-to-all-start.3 = ((bf16[2,128,256]{2,0,1:T(2,128)(2,1)}), bf16[2,128,256]{2,0,1:T(2,128)(2,1)S(1)}, u32[]{:S(2)}, u32[]{:S(2)}) async-start(bf16[2,128,256]{2,0,1:T(2,128)(2,1)} %copy.64), calls=%async_computation.3 | async-start | bytes 262144 | tf_op jit(solution)/shard_map/all_to_all | solution.py:41
  278.7 3.9 %copy-start.2 = (bf16[2,128,3584]{1,2,0:T(8,128)(2,1)S(1)}, bf16[2,128,3584]{1,2,0:T(8,128)(2,1)}, u32[]{:S(2)}) copy-start(bf16[2,128,3584]{1,2,0:T(8,128)(2,1)} %copy.70) | copy-start | bytes 5505028
  282.6 1.5 copy-start.4
  284.9 1.5 copy-start.4
  290.9 22.9 %all-to-all-start.5 = ((bf16[2,128,256]{2,0,1:T(2,128)(2,1)}), bf16[2,128,256]{2,0,1:T(2,128)(2,1)S(1)}, u32[]{:S(2)}, u32[]{:S(2)}) async-start(bf16[2,128,256]{2,0,1:T(2,128)(2,1)} %copy.72), calls=%async_computation.5 | async-start | bytes 262144 | tf_op jit(solution)/shard_map/all_to_all | solution.py:41
where the time goes:
time: 317 us; the launch traced here: 315 us
  waiting for transfers between devices  176 us (56%)
  starting transfers between devices  62.7 us (20%)
  local copies, waits for them, and re-layouts  54.2 us (17%)
  blocking collectives  10.5 us (3%)
  other arithmetic  5.92 us (2%)
    all_to_all x2, waiting for transfers between devices, shards(): lax.all_to_all(send_buffer, 'ep', split_axis=1, concat_axis=1, tiled=True)  83.6 us
    all_to_all x1, waiting for transfers between devices, shards(): lax.all_to_all(pieces, 'ep', split_axis=0, concat_axis=0, tiled=True)  44.2 us
    all_to_all x1, waiting for transfers between devices, shards(): lax.all_to_all(jnp.take(lax.all_to_all(pieces, 'ep', split_axis=0, concat...  38.2 us
    all_to_all x2, starting transfers between devices, shards(): lax.all_to_all(send_buffer, 'ep', split_axis=1, concat_axis=1, tiled=True)  28.6 us
    all_to_all x2, starting transfers between devices, serve_rows(): lax.all_to_all(activated, 'ep', split_axis=1, concat_axis=1, tiled=True)  18.5 us
    while x5, local copies, waits for them, and re-layouts, serve_rows(): activated = lax.map(one_slot, arrived)  12.7 us
    all_gather x1, blocking collectives, shards(): grouped = lax.all_gather(tokens, 'dp', axis=1, tiled=True)  10.5 us
    all_to_all x2, waiting for transfers between devices, serve_rows(): lax.all_to_all(activated, 'ep', split_axis=1, concat_axis=1, tiled=True)  10.3 us
  transfers between devices with their start and end apart: 6, of which 6 were waited for; matrix products, arithmetic and copies ran while one was open for 13% of the time, Pallas kernels for 0%

commit v1 on v0

--- a/solution.py
+++ b/solution.py
@@ -2,6 +2,7 @@
 import jax.numpy as jnp
 from jax import lax
 from jax.sharding import PartitionSpec as P
+from jax.lax import all_to_all, psum
 
 
 def inverse_place(expert_at):
@@ -74,7 +75,10 @@
     ).reshape(old_block.shape)
     first_serve = (new_block, new_expert)
     serve_plans = [first_serve] + [(new_block, new_expert)] * (tokens.shape[0] - 1)
-    grouped = lax.all_gather(tokens, "dp", axis=1, tiled=True)
+    map_the_grid = lambda ax_name, x_local: jnp.concatenate(
+        all_to_all(jnp.stack(psum(1, ax_name) * [x_local]), ax_name, 0, 0), axis=1
+    )
+    grouped = map_the_grid("dp", tokens)
     columns = grouped.shape[2]
     combined_steps = []
     for decode_step in range(tokens.shape[0]):

time: 317 us -> 306 us (0.965)
  blocking collectives: 10.5 us -> 0 us
  waiting for transfers between devices: 176 us -> 172 us
  starting transfers between devices: 62.7 us -> 66.4 us
    all_to_all x2, starting transfers between devices: 28.6 us -> 16.3 us  [shards(): lax.all_to_all(send_buffer, 'ep', split_axis=1, concat_axis=1, tiled=True)]
    all_to_all x1, starting transfers between devices: 7.79 us -> 19 us  [shards(): lax.all_to_all(pieces, 'ep', split_axis=0, concat_axis=0, tiled=True)]
    all_gather x1 -> x0, blocking collectives: 10.5 us -> none  [shards(): grouped = lax.all_gather(tokens, 'dp', axis=1, tiled=True)]
    all_to_all x0 -> x1, starting transfers between devices: none -> 4.83 us  [shards(): all_to_all(jnp.stack(psum(1, ax_name) * [x_local]), ax_name, 0, 0)]
    all_to_all x2, waiting for transfers between devices: 83.6 us -> 79.1 us  [shards(): lax.all_to_all(send_buffer, 'ep', split_axis=1, concat_axis=1, tiled=True)]
  transfers between devices with their start and end apart: 6 -> 7, of which waited for: 6 -> 7; matrix products, arithmetic and copies ran while one was open for 13% -> 16% of each run, Pallas kernels for 0% -> 0%
where the time goes in v1:
time: 306 us; the launch traced here: 305 us
  waiting for transfers between devices  172 us (56%)
  starting transfers between devices  66.4 us (22%)
  local copies, waits for them, and re-layouts  55.1 us (18%)
  other arithmetic  5.19 us (2%)
    all_to_all x2, waiting for transfers between devices, shards(): lax.all_to_all(send_buffer, 'ep', split_axis=1, concat_axis=1, tiled=True)  79.1 us
    all_to_all x1, waiting for transfers between devices, shards(): lax.all_to_all(pieces, 'ep', split_axis=0, concat_axis=0, tiled=True)  42.8 us
    all_to_all x1, waiting for transfers between devices, shards(): lax.all_to_all(jnp.take(lax.all_to_all(pieces, 'ep', split_axis=0, concat...  38.2 us
    all_to_all x1, starting transfers between devices, shards(): lax.all_to_all(pieces, 'ep', split_axis=0, concat_axis=0, tiled=True)  19 us
    all_to_all x2, starting transfers between devices, serve_rows(): lax.all_to_all(activated, 'ep', split_axis=1, concat_axis=1, tiled=True)  18.5 us
    all_to_all x2, starting transfers between devices, shards(): lax.all_to_all(send_buffer, 'ep', split_axis=1, concat_axis=1, tiled=True)  16.3 us
    while x5, local copies, waits for them, and re-layouts, serve_rows(): activated = lax.map(one_slot, arrived)  12.7 us
    all_to_all x2, waiting for transfers between devices, serve_rows(): lax.all_to_all(activated, 'ep', split_axis=1, concat_axis=1, tiled=True)  10.3 us
  transfers between devices with their start and end apart: 7, of which 7 were waited for; matrix products, arithmetic and copies ran while one was open for 16% of the time, Pallas kernels for 0%

profile of v1, /device:TPU:1, one launch (start us, length us, event | category | flops | bytes accessed | tf_op | source)
XLA Modules:
  0.0 304.6 jit_solution(17442843662168395449)
XLA Ops:
  0.6 1.6 stack.4
  2.2 4.8 %all-to-all-start = ((bf16[4,2,4,3584]{3,2,1,0:T(4,128)(2,1)}), bf16[4,2,4,3584]{3,2,1,0:T(4,128)(2,1)S(1)}, u32[]{:S(2)}, u32[]{:S(2)}) async-start(bf16[4,2,4,3584]{3,2,1,0:T(4,128)(2,1)} %stack.4), calls=%async_computation | async-start | bytes 458752 | tf_op jit(solution)/shard_map/all_to_all | solution.py:79
  7.0 3.7 %reshape_squeeze.3 = bf16[128,28,256]{2,1,0:T(8,128)(2,1)} reshape(bf16[1,3584,256]{2,1,0:T(8,128)(2,1)} %param.14) | data formatting | bytes 3670016 | tf_op jit(solution)/shard_map/reshape;squeeze | solution.py:66
  10.8 1.6 all-to-all-done
  12.4 19.0 %all-to-all-start.2 = ((bf16[128,28,256]{2,1,0:T(8,128)(2,1)}), bf16[128,28,256]{2,1,0:T(8,128)(2,1)S(1)}, u32[]{:S(2)}, u32[]{:S(2)}) async-start(bf16[128,28,256]{2,1,0:T(8,128)(2,1)} %reshape_squeeze.3), calls=%async_computation.2 | async-start | bytes 4194304 | tf_op jit(solution)/shard_map/all_to_all | solution.py:69
  31.5 0.1 eq.32
  31.7 0.1 eq.79
  31.8 0.1 fusion.21
  31.9 0.2 reduce_window_sum.17
  32.0 0.1 fusion.20
  32.1 0.2 reduce_window_sum.18
  32.3 0.2 select_reduce_fusion.2
  32.5 0.2 select_reduce_fusion.5
  32.7 0.1 fusion.25
  32.9 3.3 %scatter_custom_fusion = bf16[256,3584]{1,0:T(8,128)(2,1)} fusion(s32[128]{0:T(128)S(1)} %get-tuple-element.130, bf16[]{:T(256)} %constant.58.clone.1, bf16[16,3584]{1,0:T(8,128)(2,1)S(1)} %squeeze.17), kind=kCustom, calls=%fused_computation.26 | custom fusion | bytes 1949698 | tf_op jit(solution)/shard_map/scatter | solution.py:89
  36.2 4.6 %copy.40 = bf16[2,128,3584]{2,0,1:T(2,128)(2,1)} copy(bf16[2,128,3584]{2,1,0:T(8,128)(2,1)} %bitcast.125) | data formatting | bytes 3670016 | tf_op jit(solution)/shard_map/reshape | solution.py:90
  40.8 42.8 %all-to-all-done.2 = bf16[128,28,256]{2,1,0:T(8,128)(2,1)S(1)} async-done(((bf16[128,28,256]{2,1,0:T(8,128)(2,1)}), bf16[128,28,256]{2,1,0:T(8,128)(2,1)S(1)}, u32[]{:S(2)}, u32[]{:S(2)}) %all-to-all-start.2) | async-done | bytes 1835040 | tf_op jit(solution)/shard_map/all_to_all | solution.py:69
  83.6 8.1 %all-to-all-start.1 = ((bf16[2,128,3584]{2,0,1:T(2,128)(2,1)}), bf16[2,128,3584]{2,0,1:T(2,128)(2,1)}, u32[]{:S(2)}, u32[]{:S(2)}) async-start(bf16[2,128,3584]{2,0,1:T(2,128)(2,1)} %copy.40), calls=%async_computation.1 | async-start | bytes 3670016 | tf_op jit(solution)/shard_map/all_to_all | solution.py:93
  91.7 3.3 %scatter_custom_fusion.1 = bf16[256,3584]{1,0:T(8,128)(2,1)} fusion(s32[128]{0:T(128)S(1)} %get-tuple-element.131, bf16[]{:T(256)} %constant.58.clone.1, bf16[16,3584]{1,0:T(8,128)(2,1)S(1)} %squeeze.20), kind=kCustom, calls=%fused_computation.24 | custom fusion | bytes 1949698 | tf_op jit(solution)/shard_map/scatter | solution.py:89
  95.1 4.6 %copy.48 = bf16[2,128,3584]{2,0,1:T(2,128)(2,1)} copy(bf16[2,128,3584]{2,1,0:T(8,128)(2,1)} %bitcast.126) | data formatting | bytes 3670016 | tf_op jit(solution)/shard_map/reshape | solution.py:90
  99.7 38.2 %all-to-all-done.1 = bf16[2,128,3584]{2,0,1:T(2,128)(2,1)} async-done(((bf16[2,128,3584]{2,0,1:T(2,128)(2,1)}), bf16[2,128,3584]{2,0,1:T(2,128)(2,1)}, u32[]{:S(2)}, u32[]{:S(2)}) %all-to-all-start.1) | async-done | bytes 1835040 | tf_op jit(solution)/shard_map/all_to_all | solution.py:93
  137.9 8.2 %all-to-all-start.5 = ((bf16[2,128,3584]{2,0,1:T(2,128)(2,1)}), bf16[2,128,3584]{2,0,1:T(2,128)(2,1)}, u32[]{:S(2)}, u32[]{:S(2)}) async-start(bf16[2,128,3584]{2,0,1:T(2,128)(2,1)} %copy.48), calls=%async_computation.5 | async-start | bytes 3670016 | tf_op jit(solution)/shard_map/all_to_all | solution.py:93
  146.1 2.0 gather_fusion
  148.2 3.2 %broadcast_select_fusion = bf16[128,28,256]{2,1,0:T(8,128)(2,1)} fusion(bf16[128,28,256]{2,1,0:T(8,128)(2,1)} %gather_fusion, pred[128]{0:T(512)(128)(4,1)S(1)} %compare_and_fusion), kind=kLoop, calls=%fused_computation.23 | loop fusion | flops 917504 | bytes 3670144 | tf_op jit(solution)/shard_map/jit(_take)/select_n | solution.py:68
  151.4 40.9 %all-to-all-done.5 = bf16[2,128,3584]{2,0,1:T(2,128)(2,1)} async-done(((bf16[2,128,3584]{2,0,1:T(2,128)(2,1)}), bf16[2,128,3584]{2,0,1:T(2,128)(2,1)}, u32[]{:S(2)}, u32[]{:S(2)}) %all-to-all-start.5) | async-done | bytes 1835040 | tf_op jit(solution)/shard_map/all_to_all | solution.py:93
  192.3 7.8 %all-to-all-start.3 = ((bf16[128,28,256]{2,1,0:T(8,128)(2,1)}), bf16[128,28,256]{2,1,0:T(8,128)(2,1)S(1)}, u32[]{:S(2)}, u32[]{:S(2)}) async-start(bf16[128,28,256]{2,1,0:T(8,128)(2,1)} %broadcast_select_fusion), calls=%async_computation.3 | async-start | bytes 4194304 | tf_op jit(solution)/shard_map/all_to_all | solution.py:67
  200.1 0.6 dynamic_slice.15
  202.6 0.1 constant_dynamic-slice_fusion.2
  202.7 0.1 copy.41
  202.8 0.1 copy.43
  202.9 5.6 %copy.42 = bf16[2,128,3584]{1,2,0:T(8,128)(2,1)} copy(bf16[2,128,3584]{2,0,1:T(2,128)(2,1)} %all-to-all-done.1) | data formatting | bytes 3670016 | tf_op jit(solution)/shard_map/while | solution.py:41
  208.5 5.5 %copy.49 = bf16[2,128,3584]{1,2,0:T(8,128)(2,1)} copy(bf16[2,128,3584]{2,0,1:T(2,128)(2,1)} %all-to-all-done.5) | data formatting | bytes 3670016 | tf_op jit(solution)/shard_map/while | solution.py:41
  214.0 38.2 %all-to-all-done.3 = bf16[128,28,256]{2,1,0:T(8,128)(2,1)S(1)} async-done(((bf16[128,28,256]{2,1,0:T(8,128)(2,1)}), bf16[128,28,256]{2,1,0:T(8,128)(2,1)S(1)}, u32[]{:S(2)}, u32[]{:S(2)}) %all-to-all-start.3) | async-done | bytes 1835040 | tf_op jit(solution)/shard_map/all_to_all | solution.py:67
  252.2 1.5 reshape_reshape.6
  253.7 0.4 copy-done.1
  254.1 5.2 %while.22 = (s32[]{:T(128)}, bf16[2,128,256]{2,1,0:T(8,128)(2,1)S(1)}, bf16[2,128,3584]{1,2,0:T(8,128)(2,1)}, bf16[128,28,256]{2,1,0:T(8,128)(2,1)}, f32[28,2]{1...) while((s32[]{:T(128)}, bf16[2,128,256]{2,1,0:T(8,128)(2,1)S(1)}, ...), condition=%wide.wide.region_8.9_spmd, body=%wide.wide.region_6.8_spmd.sunk | while | flops 236847104 | bytes 12439901 | solution.py:41
  254.1 1.4 constant_dynamic-slice_fusion.7
  255.5 0.1 broadcast_in_dim.76
  255.6 0.3 copy-done.4
  255.9 0.7 multiply_reduce_fusion.6
  256.7 1.4 constant_dynamic-slice_fusion.7
  258.1 0.1 broadcast_in_dim.76
  258.2 0.3 copy-done.4
  258.5 0.7 multiply_reduce_fusion.6
  259.3 0.8 copy.44
  260.1 7.7 %all-to-all-start.4 = ((bf16[2,128,256]{2,0,1:T(2,128)(2,1)}), bf16[2,128,256]{2,0,1:T(2,128)(2,1)S(1)}, u32[]{:S(2)}, u32[]{:S(2)}) async-start(bf16[2,128,256]{2,0,1:T(2,128)(2,1)} %copy.44), calls=%async_computation.4 | async-start | bytes 262144 | tf_op jit(solution)/shard_map/all_to_all | solution.py:42
  267.8 3.9 %reshape_reshape.8 = bf16[28,128,256]{2,1,0:T(8,128)(2,1)} reshape(bf16[128,28,256]{2,1,0:T(8,128)(2,1)} %get-tuple-element.295) | data formatting | bytes 3670016 | tf_op jit(solution)/shard_map/while/body/eval_jaxpr/reshape;reshape | solution.py:27
  271.7 4.6 %while.23 = (s32[]{:T(128)}, bf16[2,128,256]{2,1,0:T(8,128)(2,1)S(1)}, bf16[2,128,3584]{1,2,0:T(8,128)(2,1)S(1)}, bf16[128,28,256]{2,1,0:T(8,128)(2,1)}, f32[28,...) while((s32[]{:T(128)}, bf16[2,128,256]{2,1,0:T(8,128)(2,1)S(1)}, ...), condition=%wide.wide.region_16.17_spmd, body=%wide.wide.region_14.16_spmd.sunk | while | flops 236847104 | bytes 12439901 | solution.py:41
  271.8 0.1 broadcast_in_dim.77
  271.9 1.3 copy-done.3
  273.2 0.7 multiply_reduce_fusion.7
  274.1 0.1 broadcast_in_dim.77
  274.2 1.3 copy-done.3
  275.5 0.7 multiply_reduce_fusion.7
  276.3 0.8 copy.51
  277.1 3.0 all-to-all-done.4
  280.1 10.8 %all-to-all-start.6 = ((bf16[2,128,256]{2,0,1:T(2,128)(2,1)}), bf16[2,128,256]{2,0,1:T(2,128)(2,1)S(1)}, u32[]{:S(2)}, u32[]{:S(2)}) async-start(bf16[2,128,256]{2,0,1:T(2,128)(2,1)} %copy.51), calls=%async_computation.6 | async-start | bytes 262144 | tf_op jit(solution)/shard_map/all_to_all | solution.py:42
  291.0 3.7 %broadcast_in_dim_reshape.3 = bf16[1,3584,256]{2,1,0:T(8,128)(2,1)} reshape(bf16[128,28,256]{2,1,0:T(8,128)(2,1)} %get-tuple-element.296) | data formatting | bytes 3670016 | tf_op jit(solution)/shard_map/broadcast_in_dim;reshape | solution.py:99
  294.8 0.8 gather_fusion.1
  295.6 0.1 fusion.19
  295.7 7.3 %all-to-all-done.6 = bf16[2,128,256]{2,0,1:T(2,128)(2,1)S(1)} async-done(((bf16[2,128,256]{2,0,1:T(2,128)(2,1)}), bf16[2,128,256]{2,0,1:T(2,128)(2,1)S(1)}, u32[]{:S(2)}, u32[]{:S(2)}) %all-to-all-start.6) | async-done | bytes 131104 | tf_op jit(solution)/shard_map/all_to_all | solution.py:42
  303.0 0.8 gather_fusion.2
  303.9 0.1 fusion.18
  304.0 0.6 pad_maximum_fusion
  (49 shorter events, 0.9 us)
Async XLA Ops:
  0.6 202.0 %copy-start = (f32[128,28,2]{0,2,1:T(2,128)S(1)}, f32[128,28,2]{0,2,1:T(2,128)}, u32[]{:S(2)}) copy-start(f32[128,28,2]{0,2,1:T(2,128)} %param.15) | copy-start | bytes 86020
  2.2 10.2 %all-to-all-start = ((bf16[4,2,4,3584]{3,2,1,0:T(4,128)(2,1)}), bf16[4,2,4,3584]{3,2,1,0:T(4,128)(2,1)S(1)}, u32[]{:S(2)}, u32[]{:S(2)}) async-start(bf16[4,2,4,3584]{3,2,1,0:T(4,128)(2,1)} %stack.4), calls=%async_computation | async-start | bytes 458752 | tf_op jit(solution)/shard_map/all_to_all | solution.py:79
  10.8 20.6 %copy-start.5 = (s32[2,16,8]{1,2,0:T(8,128)S(1)}, s32[2,16,8]{1,2,0:T(8,128)}, u32[]{:S(2)}) copy-start(s32[2,16,8]{1,2,0:T(8,128)} %param.12) | copy-start | bytes 3076
  10.8 21.5 %copy-start.7 = (s32[128]{0:T(128)S(1)}, s32[128]{0:T(128)}, u32[]{:S(2)}) copy-start(s32[128]{0:T(128)} %param.17) | copy-start | bytes 1540
  10.8 21.5 %copy-start.8 = (s32[128]{0:T(128)S(1)}, s32[128]{0:T(128)}, u32[]{:S(2)}) copy-start(s32[128]{0:T(128)} %param.16) | copy-start | bytes 1540
  12.4 71.2 %all-to-all-start.2 = ((bf16[128,28,256]{2,1,0:T(8,128)(2,1)}), bf16[128,28,256]{2,1,0:T(8,128)(2,1)S(1)}, u32[]{:S(2)}, u32[]{:S(2)}) async-start(bf16[128,28,256]{2,1,0:T(8,128)(2,1)} %reshape_squeeze.3), calls=%async_computation.2 | async-start | bytes 4194304 | tf_op jit(solution)/shard_map/all_to_all | solution.py:69
  83.6 54.3 %all-to-all-start.1 = ((bf16[2,128,3584]{2,0,1:T(2,128)(2,1)}), bf16[2,128,3584]{2,0,1:T(2,128)(2,1)}, u32[]{:S(2)}, u32[]{:S(2)}) async-start(bf16[2,128,3584]{2,0,1:T(2,128)(2,1)} %copy.40), calls=%async_computation.1 | async-start | bytes 3670016 | tf_op jit(solution)/shard_map/all_to_all | solution.py:93
  137.9 54.4 %all-to-all-start.5 = ((bf16[2,128,3584]{2,0,1:T(2,128)(2,1)}), bf16[2,128,3584]{2,0,1:T(2,128)(2,1)}, u32[]{:S(2)}, u32[]{:S(2)}) async-start(bf16[2,128,3584]{2,0,1:T(2,128)(2,1)} %copy.48), calls=%async_computation.5 | async-start | bytes 3670016 | tf_op jit(solution)/shard_map/all_to_all | solution.py:93
  151.4 51.5 %copy-start.6 = (f32[2,16,8]{1,2,0:T(8,128)S(1)}, f32[2,16,8]{1,2,0:T(8,128)}, u32[]{:S(2)}) copy-start(f32[2,16,8]{1,2,0:T(8,128)} %param.13) | copy-start | bytes 3076
  192.3 59.9 %all-to-all-start.3 = ((bf16[128,28,256]{2,1,0:T(8,128)(2,1)}), bf16[128,28,256]{2,1,0:T(8,128)(2,1)S(1)}, u32[]{:S(2)}, u32[]{:S(2)}) async-start(bf16[128,28,256]{2,1,0:T(8,128)(2,1)} %broadcast_select_fusion), calls=%async_computation.3 | async-start | bytes 4194304 | tf_op jit(solution)/shard_map/all_to_all | solution.py:67
  252.2 1.9 copy-start.1
  254.1 1.8 copy-start.4
  256.7 1.8 copy-start.4
  260.1 20.0 %all-to-all-start.4 = ((bf16[2,128,256]{2,0,1:T(2,128)(2,1)}), bf16[2,128,256]{2,0,1:T(2,128)(2,1)S(1)}, u32[]{:S(2)}, u32[]{:S(2)}) async-start(bf16[2,128,256]{2,0,1:T(2,128)(2,1)} %copy.44), calls=%async_computation.4 | async-start | bytes 262144 | tf_op jit(solution)/shard_map/all_to_all | solution.py:42
  267.8 3.9 %copy-start.2 = (bf16[2,128,3584]{1,2,0:T(8,128)(2,1)S(1)}, bf16[2,128,3584]{1,2,0:T(8,128)(2,1)}, u32[]{:S(2)}) copy-start(bf16[2,128,3584]{1,2,0:T(8,128)(2,1)} %copy.49) | copy-start | bytes 5505028
  271.7 1.5 copy-start.3
  274.0 1.5 copy-start.3
  280.1 22.9 %all-to-all-start.6 = ((bf16[2,128,256]{2,0,1:T(2,128)(2,1)}), bf16[2,128,256]{2,0,1:T(2,128)(2,1)S(1)}, u32[]{:S(2)}, u32[]{:S(2)}) async-start(bf16[2,128,256]{2,0,1:T(2,128)(2,1)} %copy.51), calls=%async_computation.6 | async-start | bytes 262144 | tf_op jit(solution)/shard_map/all_to_all | solution.py:42
